TPU v7x, 32 devices: a whole 2x2x4 slice. The times are simulated.
32 devices in a mesh: groups: 2 (over y), col: 4 (over z), aux: 2 (over x), rep: 2 (over core).
Axes of the slice: x: 2, y: 2, z: 4, core: 2. Of those that a mesh axis runs over, the one named last changes fastest.
Arguments:
- b_aux: bfloat16 [4, 4096, 2400], P(('groups', 'aux'), ('col', 'rep')), parts along dimension 0, may hold values from -0.59765625 to 0.59765625
- occ_energies: float32 [2], P('groups'), parts along dimension 0, may hold values from -2 to -0.3
- vir_energies: float32 [4800], P('groups'), parts along dimension 0, may hold values from 0.2 to 3
- owners: int32 [2], replicated, may hold values from 0 to 7
Outputs:
- gamma: float32 [4, 4096, 2400], P(('groups', 'aux'), None, ('col', 'rep')), parts along dimension 0
There are 2 independent parts, one for each index of `groups`. A program takes and returns all parts, laid end to end along the dimension named above; an argument that names none is the same for every part. Nothing has to cross between parts.
Inputs may be any that keep to these rules, and one draw needn't show every extreme that they name: owners[s] is a column shard index in the order of col+rep; owners may repeat.
All inputs are finite; a program needn't handle non-finite values.
Results may differ from a plain program's by a relative error of at most 0.003.
Values may be sent and summed in bfloat16 or wider, within the bound.
No kernel may reach another device: no remote copies, remote signals or barrier semaphores. Data moves between devices by JAX's collectives and lax.ppermute only.
A program may use at most 64 MiB of HBM per device.

v0:
```python
import jax
import jax.numpy as jnp
from jax import lax
from jax.sharding import PartitionSpec as P

os_scale = 1.3


def from_root(value, axis, source):
    kept = jnp.where(lax.axis_index(axis) == source, value, 0).astype(value.dtype)
    return lax.psum(kept, axis)


def column_energy(first, occ_energies, vir_energies, width):
    nvirt = vir_energies.shape[0]
    occ_value = lax.dynamic_index_in_dim(occ_energies, first // nvirt, 0, keepdims=False)
    vir_values = lax.dynamic_slice_in_dim(vir_energies, first % nvirt, width, 0)
    return vir_values - occ_value


def body(b_aux, occ_energies, vir_energies, owners):
    moved = lax.all_to_all(b_aux, ("col", "rep"), split_axis=2, concat_axis=1, tiled=True)
    local_cols = moved[0]
    width = local_cols.shape[1]
    shard_index = lax.axis_index(("col", "rep"))
    energy_mine = column_energy(shard_index * width, occ_energies, vir_energies, width)
    gamma_acc = jnp.zeros(local_cols.shape, jnp.float32)
    for step_index in range(owners.shape[0]):
        owner_shard = owners[step_index]
        owner_cols = from_root(local_cols, ("col", "rep"), owner_shard)
        owner_energy = column_energy(owner_shard * width, occ_energies, vir_energies, width)
        denominator = energy_mine[:, None] + owner_energy[None, :]
        partial_value = lax.dot_general(
            local_cols, owner_cols, (((0,), (0,)), ((), ())), preferred_element_type=jnp.float32
        )
        coupling = lax.psum(partial_value, "aux")
        amplitude = (os_scale * coupling / denominator).astype(jnp.bfloat16)
        gamma_acc = gamma_acc + lax.dot_general(
            owner_cols, amplitude, (((1,), (1,)), ((), ())), preferred_element_type=jnp.float32
        )
    return gamma_acc[None]


def solution(mesh):
    placed = (P(("groups", "aux"), ("col", "rep"), None), P("groups"), P("groups"), P())
    return jax.shard_map(
        body,
        mesh=mesh,
        in_specs=placed,
        out_specs=P(("groups", "aux"), None, ("col", "rep")),
        check_vma=False,
    )
```

profile of v0, /device:TPU:0, one launch (start us, length us, event | category | flops | bytes accessed | tf_op | source)
XLA Modules:
  0.0 311.1 jit_solution(7487857900732730221)
XLA Ops:
  6.5 13.4 %copy.16 = bf16[1,512,2400]{1,0,2:T(2,128)(2,1)} copy(bf16[1,512,2400]{1,2,0:T(8,128)(2,1)} %param.4) | data formatting | bytes 4915200 | tf_op args[0]
  20.0 0.6 broadcast.16
  20.6 16.3 %reduce.2 = bf16[2400,512]{1,0:T(8,128)(2,1)S(1)} reduce(bf16[2400,1,512]{2,1,0:T(2,128)(2,1)} %bitcast.32, bf16[]{:T(256)} %broadcast.16), dimensions={1}, to_apply=%bitcast.30.reduce_sub_computation | reduce | bytes 4915202
  36.9 2.4 reshape.5
  39.3 0.0 copy-start.4
  39.3 6.5 %all-to-all-start = ((bf16[8,2,76800]{2,1,0:T(2,128)(2,1)}), bf16[8,2,76800]{2,1,0:T(2,128)(2,1)S(1)}, u32[]{:S(2)}, u32[]{:S(2)}) async-start(bf16[8,2,76800]{2,1,0:T(2,128)(2,1)} %reshape.5), calls=%async_computation | async-start | bytes 4915200 | tf_op jit(solution)/shard_map/all_to_all | solution.py:22
  45.7 0.0 all-reduce.7.cloned.1.call-start
  45.8 0.0 copy-done.4
  45.8 0.6 fusion.10
  47.7 54.8 %all-to-all-done = bf16[8,2,76800]{2,1,0:T(2,128)(2,1)S(1)} async-done(((bf16[8,2,76800]{2,1,0:T(2,128)(2,1)}), bf16[8,2,76800]{2,1,0:T(2,128)(2,1)S(1)}, u32[]{:S(2)}, u32[]{:S(2)}) %all-to-all-start) | async-done | bytes 2457632 | tf_op jit(solution)/shard_map/all_to_all | solution.py:22
  102.5 4.4 %reshape.6 = bf16[2400,1,512]{2,1,0:T(2,128)(2,1)} reshape(bf16[8,2,76800]{2,1,0:T(2,128)(2,1)S(1)} %all-to-all-done) | data formatting | bytes 4915200
  107.0 17.2 %bitcast_reduce_fusion = bf16[512,2400]{0,1:T(8,128)(2,1)} fusion(bf16[2400,1,512]{2,1,0:T(2,128)(2,1)} %reshape.6), kind=kLoop, calls=%fused_computation.22 | loop fusion | bytes 4915200 | tf_op jit(solution)/shard_map/all_to_all | solution.py:22
  124.1 2.6 all_to_all.12
  126.8 1.4 copy.15
  128.1 0.2 pad
  128.3 1.1 copy.12
  129.4 2.6 broadcast_select_fusion
  132.1 0.0 all-reduce.7.cloned.1.call-update
  132.1 0.2 all-reduce.5.cloned.1.call-start
  132.3 110.6 %all-reduce.7.cloned.1.call-done = (bf16[4096,300]{0,1:T(8,128)(2,1)}, bf16[4096,300]{0,1:T(8,128)(2,1)}) async-done(((bf16[4096,300]{0,1:T(8,128)(2,1)}, bf16[4096,300]{0,1:T(8,128)(2,1)}), (bf16[4096,300]{0,1:T(8,128)(2,1)}, bf16[4096,300]{0,1:T(8,128)(2,1)})) %all-reduce.7.cloned.1.call-update) | async-done | bytes 4915216 | tf_op jit(solution)/shard_map/psum | solution.py:11
  242.9 0.0 copy-start
  242.9 4.1 %convolution_bitcast_fusion.1 = f32[300,300]{0,1:T(8,128)} fusion(bf16[4096,300]{0,1:T(8,128)(2,1)} %get-tuple-element.7, bf16[4096,300]{0,1:T(8,128)(2,1)S(1)} %bitcast.34), kind=kOutput, calls=%fused_computation.6 | convolution fusion | flops 737280000 | bytes 5275200 | tf_op jit(solution)/shard_map/dot_general | solution.py:33
  247.0 0.0 copy-done
  247.0 0.0 copy-start.3
  247.0 2.3 convolution_bitcast_fusion
  249.2 0.0 all-reduce.5.cloned.1.call-update
  251.2 0.0 copy-done.3
  251.2 0.1 dynamic-slice_subtract_fusion
  251.3 35.9 %all-reduce.5.cloned.1.call-done = (f32[300,300]{0,1:T(8,128)}, f32[300,300]{0,1:T(8,128)}) async-done(((f32[300,300]{0,1:T(8,128)}, f32[300,300]{0,1:T(8,128)}), (f32[300,300]{0,1:T(8,128)}, f32[300,300]{0,1:T(8,128)})) %all-reduce.5.cloned.1.call-update) | async-done | bytes 720016 | tf_op jit(solution)/shard_map/psum | solution.py:36
  287.2 0.0 copy-start.1
  287.2 0.0 copy-start.2
  287.2 3.5 %fusion.1 = f32[4096,300]{0,1:T(8,128)S(1)} fusion(bf16[4096,300]{0,1:T(8,128)(2,1)} %get-tuple-element.7, f32[300,300]{0,1:T(8,128)} %get-tuple-element.5, f32[300]{0:T(512)S(1)} %get-tuple-element.13, f32[300]{0:T(512)S(1)} %get-tuple-element.12), kind=kOutput, calls=%fused_computation.9 | convolution fusion | flops 737640000 | bytes 7735200 | tf_op jit(solution)/shard_map/dot_general | solution.py:38
  290.7 0.0 copy-done.1
  290.7 0.0 copy-done.2
  290.7 3.9 %fusion = f32[1,4096,300]{1,2,0:T(8,128)} fusion(f32[4096,300]{0,1:T(8,128)S(1)} %fusion.1, bf16[4096,300]{0,1:T(8,128)(2,1)S(1)} %copy-done.1, f32[300,300]{0,1:T(8,128)S(1)} %copy-done.2, f32[300]{0:T(512)S(1)} %get-tuple-element.11, f32[300]{0:T(512)S(1)} %get-tuple-element.12), kind=kOutput, calls=%fused_computation.1 | convolution fusion | flops 738868800 | bytes 12650400 | tf_op jit(solution)/shard_map/dot_general | solution.py:38
  294.6 9.7 %copy.10 = f32[1,4096,300]{1,0,2:T(1,128)} copy(f32[1,4096,300]{1,2,0:T(8,128)} %fusion) | data formatting | bytes 9830400 | tf_op jit(solution)/shard_map/broadcast_in_dim | solution.py:41
Async XLA Ops:
  39.3 6.5 %copy-start.4 = (s32[2]{0:T(128)S(1)}, s32[2]{0:T(128)}, u32[]{:S(2)}) copy-start(s32[2]{0:T(128)} %param.7) | copy-start | bytes 28
  39.3 63.2 %all-to-all-start = ((bf16[8,2,76800]{2,1,0:T(2,128)(2,1)}), bf16[8,2,76800]{2,1,0:T(2,128)(2,1)S(1)}, u32[]{:S(2)}, u32[]{:S(2)}) async-start(bf16[8,2,76800]{2,1,0:T(2,128)(2,1)} %reshape.5), calls=%async_computation | async-start | bytes 4915200 | tf_op jit(solution)/shard_map/all_to_all | solution.py:22
  45.7 197.1 %all-reduce.7.cloned.1.call-start = ((), (), s32[]{:S(2)}) async-start(), calls=%async_computation.2 | async-start | bytes 9961472 | tf_op jit(solution)/shard_map/psum | solution.py:11
  132.1 155.1 %all-reduce.5.cloned.1.call-start = ((), (), s32[]{:S(2)}) async-start(), calls=%async_computation.1 | async-start | bytes 1867776 | tf_op jit(solution)/shard_map/psum | solution.py:36
  242.9 4.1 %copy-start = (bf16[4096,300]{0,1:T(8,128)(2,1)S(1)}, bf16[4096,300]{0,1:T(8,128)(2,1)}, u32[]{:S(2)}) copy-start(bf16[4096,300]{0,1:T(8,128)(2,1)} %get-tuple-element.8) | copy-start | bytes 7372804
  247.0 4.2 %copy-start.3 = (f32[2400]{0:T(1024)S(1)}, f32[2400]{0:T(1024)}, u32[]{:S(2)}) copy-start(f32[2400]{0:T(1024)} %param.6) | copy-start | bytes 28804
  287.2 3.5 %copy-start.1 = (bf16[4096,300]{0,1:T(8,128)(2,1)S(1)}, bf16[4096,300]{0,1:T(8,128)(2,1)}, u32[]{:S(2)}) copy-start(bf16[4096,300]{0,1:T(8,128)(2,1)} %get-tuple-element.8) | copy-start | bytes 7372804
  287.2 3.5 %copy-start.2 = (f32[300,300]{0,1:T(8,128)S(1)}, f32[300,300]{0,1:T(8,128)}, u32[]{:S(2)}) copy-start(f32[300,300]{0,1:T(8,128)} %get-tuple-element.6) | copy-start | bytes 1080004
Sparse Core Ops, SparseCore 0:
  132.2 110.6 all-reduce.6
  249.4 37.7 all-reduce.4
where the time goes:
time: 312 us; the launch traced here: 311 us
  waiting for transfers between devices  201 us (64%)
  local copies, waits for them, and re-layouts  53.6 us (17%)
  other arithmetic  19.1 us (6%)
  between operations  16.7 us (5%)
  matrix products  13.7 us (4%)
  starting transfers between devices  6.72 us (2%)
    psum x1, waiting for transfers between devices, from_root(): return lax.psum(kept, axis)  111 us
    all_to_all x1, waiting for transfers between devices, body(): lax.all_to_all(b_aux, ('col', 'rep'), split_axis=2, concat_axis=1, tiled=...  54.8 us
    psum x1, waiting for transfers between devices, body(): coupling = lax.psum(partial_value, 'aux')  35.9 us
    unnamed x16, local copies, waits for them, and re-layouts  22.1 us
    all_to_all x3, local copies, waits for them, and re-layouts, body(): lax.all_to_all(b_aux, ('col', 'rep'), split_axis=2, concat_axis=1, tiled=...  21.1 us
    unnamed x1, other arithmetic  16.3 us
    broadcast_in_dim x1, local copies, waits for them, and re-layouts, body(): return gamma_acc[None]  9.71 us
    dot_general x2, matrix products, body(): lax.dot_general(owner_cols, amplitude, (((1,), (1,)), ((), ())), preferre...  7.4 us
  transfers between devices with their start and end apart: 3, of which 3 were waited for; matrix products, arithmetic and copies ran while one was open for 0% of the time, Pallas kernels for 0%

commit v1 on v0

--- a/solution.py
+++ b/solution.py
@@ -4,6 +4,22 @@
 from jax.sharding import PartitionSpec as P
 
 os_scale = 1.3
+
+
+def exchange_in_pairs(x, axis, split, join):
+    ways, here = (lax.axis_size(axis), lax.axis_index(axis))
+    width = x.shape[split] // ways
+    shape = list(x.shape)
+    shape[split] = width
+    height = shape[join]
+    shape[join] = height * ways
+    full = jnp.zeros(shape, x.dtype)
+    for mask in range(ways):
+        part = lax.dynamic_slice_in_dim(x, (here ^ mask) * width, width, axis=split)
+        if mask:
+            part = lax.ppermute(part, axis, [(d, d ^ mask) for d in range(ways)])
+        full = lax.dynamic_update_slice_in_dim(full, part, (here ^ mask) * height, axis=join)
+    return full
 
 
 def from_root(value, axis, source):
@@ -19,7 +35,7 @@
 
 
 def body(b_aux, occ_energies, vir_energies, owners):
-    moved = lax.all_to_all(b_aux, ("col", "rep"), split_axis=2, concat_axis=1, tiled=True)
+    moved = exchange_in_pairs(b_aux, ("col", "rep"), 2, 1)
     local_cols = moved[0]
     width = local_cols.shape[1]
     shard_index = lax.axis_index(("col", "rep"))

time: 312 us -> 253 us (0.81)
  local copies, waits for them, and re-layouts: 53.6 us -> 19.7 us
  other arithmetic: 19.1 us -> 2.72 us
  waiting for transfers between devices: 201 us -> 190 us
  starting transfers between devices: 6.72 us -> 10.4 us
    all_to_all x1 -> x0, waiting for transfers between devices: 54.8 us -> none  [body(): lax.all_to_all(b_aux, ('col', 'rep'), split_axis=2, concat_axis=1, tiled=...]
    ppermute x0 -> x7, waiting for transfers between devices: none -> 28 us  [exchange_in_pairs(): part = lax.ppermute(part, axis, [(d, d ^ mask) for d in range(ways)])]
    unnamed x16 -> x10, local copies, waits for them, and re-layouts: 22.1 us -> 0.02 us
    all_to_all x3 -> x0, local copies, waits for them, and re-layouts: 21.1 us -> none  [body(): lax.all_to_all(b_aux, ('col', 'rep'), split_axis=2, concat_axis=1, tiled=...]
    unnamed x1 -> x0, other arithmetic: 16.3 us -> none
    psum x1, waiting for transfers between devices: 111 us -> 126 us  [from_root(): return lax.psum(kept, axis)]
    ppermute x0 -> x7, starting transfers between devices: none -> 10.2 us  [exchange_in_pairs(): part = lax.ppermute(part, axis, [(d, d ^ mask) for d in range(ways)])]
    all_to_all x1 -> x0, starting transfers between devices: 6.46 us -> none  [body(): lax.all_to_all(b_aux, ('col', 'rep'), split_axis=2, concat_axis=1, tiled=...]
  transfers between devices with their start and end apart: 3 -> 9, of which waited for: 3 -> 6; matrix products, arithmetic and copies ran while one was open for 0% -> 3% of each run, Pallas kernels for 0% -> 0%
where the time goes in v1:
time: 253 us
  waiting for transfers between devices  190 us (75%)
  local copies, waits for them, and re-layouts  19.7 us (8%)
  between operations  16.6 us (7%)
  matrix products  13.6 us (5%)
  starting transfers between devices  10.4 us (4%)
  other arithmetic  2.72 us (1%)
    psum x1, waiting for transfers between devices, from_root(): return lax.psum(kept, axis)  126 us
    psum x1, waiting for transfers between devices, body(): coupling = lax.psum(partial_value, 'aux')  35.9 us
    ppermute x7, waiting for transfers between devices, exchange_in_pairs(): part = lax.ppermute(part, axis, [(d, d ^ mask) for d in range(ways)])  28 us
    ppermute x7, starting transfers between devices, exchange_in_pairs(): part = lax.ppermute(part, axis, [(d, d ^ mask) for d in range(ways)])  10.2 us
    broadcast_in_dim x1, local copies, waits for them, and re-layouts, body(): return gamma_acc[None]  9.71 us
    dot_general x2, matrix products, body(): lax.dot_general(owner_cols, amplitude, (((1,), (1,)), ((), ())), preferre...  7.23 us
    dot_general x2, matrix products, body(): lax.dot_general(local_cols, owner_cols, (((0,), (0,)), ((), ())), preferr...  6.33 us
    dynamic_update_slice x8, local copies, waits for them, and re-layouts, exchange_in_pairs(): lax.dynamic_update_slice_in_dim(full, part, (here ^ mask) * height, axis=...  6.1 us
  transfers between devices with their start and end apart: 9, of which 6 were waited for; matrix products, arithmetic and copies ran while one was open for 3% of the time, Pallas kernels for 0%

profile of v1, /device:TPU:0, one launch (start us, length us, event | category | flops | bytes accessed | tf_op | source)
XLA Modules:
  0.0 252.7 jit_solution(12054946189291600071)
XLA Ops:
  6.5 0.0 copy-start.4
  6.5 0.0 all-reduce.7.cloned.1.call-start
  6.5 3.0 %constant_dynamic-slice_fusion = (bf16[1,512,300]{1,2,0:T(8,128)(2,1)S(1)}, bf16[1,512,300]{1,2,0:T(8,128)(2,1)S(1)}, bf16[1,512,300]{1,2,0:T(8,128)(2,1)}, bf16...) fusion(bf16[1,512,2400]{1,2,0:T(8,128)(2,1)} %param.4, ...), kind=kLoop, calls=%fused_computation.21 | loop fusion | bytes 4300828 | tf_op jit(solution)/shard_map/dynamic_slice | solution.py:18
  9.5 0.5 collective-permute-start
  10.0 2.6 %collective-permute-start.1 = (bf16[1,512,300]{1,2,0:T(8,128)(2,1)}, bf16[1,512,300]{1,2,0:T(8,128)(2,1)}, u32[]{:S(2)}, u32[]{:S(2)}) collective-permute-start(bf16[1,512,300]{1,2,0:T(8,128)(2,1)} %get-tuple-element.15), channel_id=1, source_target_pairs={{0,4},{1,5},{4,0},{5,1},{8,12},{9,13},{12,8},{13,9},{2,6},{3,7},{6... | collective-permute-start | bytes 921608 | tf_op jit(solution)/shard_map/ppermute | solution.py:20
  12.6 0.1 collective-permute-start.2
  12.7 2.7 %collective-permute-start.3 = (bf16[1,512,300]{1,2,0:T(8,128)(2,1)}, bf16[1,512,300]{1,2,0:T(8,128)(2,1)}, u32[]{:S(2)}, u32[]{:S(2)}) collective-permute-start(bf16[1,512,300]{1,2,0:T(8,128)(2,1)} %get-tuple-element.13), channel_id=1, source_target_pairs={{0,8},{1,9},{4,12},{5,13},{8,0},{9,1},{12,4},{13,5},{2,10},{3,11},... | collective-permute-start | bytes 921608 | tf_op jit(solution)/shard_map/ppermute | solution.py:20
  15.4 0.0 collective-permute-start.4
  15.4 0.0 copy-done.4
  15.4 0.6 fusion.10
  17.3 0.3 squeeze.32
  17.6 1.1 bitcast_dynamic-update-slice_fusion.7
  18.6 0.0 collective-permute-done
  18.6 3.6 %collective-permute-start.5 = (bf16[1,512,300]{1,2,0:T(8,128)(2,1)S(1)}, bf16[1,512,300]{1,2,0:T(8,128)(2,1)S(1)}, u32[]{:S(2)}, u32[]{:S(2)}) collective-permute-start(bf16[1,512,300]{1,2,0:T(8,128)(2,1)S(1)} %get-tuple-element.17), channel_id=1, source_target_pairs={{0,12},{1,13},{4,8},{5,9},{8,4},{9,5},{12,0},{13,1},{2,14},{3,15},... | collective-permute-start | bytes 921608 | tf_op jit(solution)/shard_map/ppermute | solution.py:20
  22.2 1.0 bitcast_dynamic-update-slice_fusion.6
  23.2 10.7 %collective-permute-done.1 = bf16[1,512,300]{1,2,0:T(8,128)(2,1)} collective-permute-done((bf16[1,512,300]{1,2,0:T(8,128)(2,1)}, bf16[1,512,300]{1,2,0:T(8,128)(2,1)}, u32[]{:S(2)}, u32[]{:S(2)}) %collective-permute-start.1) | collective-permute-done | bytes 307232 | tf_op jit(solution)/shard_map/ppermute | solution.py:20
  33.9 0.7 collective-permute-start.6
  34.6 1.0 bitcast_dynamic-update-slice_fusion.5
  35.7 4.6 %collective-permute-done.2 = bf16[1,512,300]{1,2,0:T(8,128)(2,1)} collective-permute-done((bf16[1,512,300]{1,2,0:T(8,128)(2,1)}, bf16[1,512,300]{1,2,0:T(8,128)(2,1)}, u32[]{:S(2)}, u32[]{:S(2)}) %collective-permute-start.2) | collective-permute-done | bytes 307232 | tf_op jit(solution)/shard_map/ppermute | solution.py:20
  40.3 1.0 bitcast_dynamic-update-slice_fusion.4
  41.3 0.0 collective-permute-done.3
  41.3 1.0 bitcast_dynamic-update-slice_fusion.3
  42.3 0.0 collective-permute-done.4
  42.3 1.0 bitcast_dynamic-update-slice_fusion.2
  43.3 6.9 %collective-permute-done.5 = bf16[1,512,300]{1,2,0:T(8,128)(2,1)S(1)} collective-permute-done((bf16[1,512,300]{1,2,0:T(8,128)(2,1)S(1)}, bf16[1,512,300]{1,2,0:T(8,128)(2,1)S(1)}, u32[]{:S(2)}, u32[]{:S(2)}) %collective-permute-start.5) | collective-permute-done | bytes 307232 | tf_op jit(solution)/shard_map/ppermute | solution.py:20
  50.2 5.9 %collective-permute-done.6 = bf16[1,512,300]{1,2,0:T(8,128)(2,1)S(1)} collective-permute-done((bf16[1,512,300]{1,2,0:T(8,128)(2,1)S(1)}, bf16[1,512,300]{1,2,0:T(8,128)(2,1)S(1)}, u32[]{:S(2)}, u32[]{:S(2)}) %collective-permute-start.6) | collective-permute-done | bytes 307232 | tf_op jit(solution)/shard_map/ppermute | solution.py:20
  56.1 2.6 %broadcast_select_fusion.1 = (bf16[4096,300]{0,1:T(8,128)(2,1)}, bf16[4096,300]{0,1:T(8,128)(2,1)}) fusion(bf16[4096,300]{0,1:T(8,128)(2,1)S(1)} %bitcast_dynamic-update-slice_fusion, pred[]{:T(512)S(6)} %eq.10, pred[]{:T(512)S(6)} %eq.11), kind=kLoop, calls=%fused_computation.3 | loop fusion | flops 2457600 | bytes 7372802 | tf_op jit(solution)/shard_map/jit(_where)/select_n | solution.py:26
  58.7 0.0 all-reduce.7.cloned.1.call-update
  58.7 0.2 all-reduce.5.cloned.1.call-start
  59.0 125.7 %all-reduce.7.cloned.1.call-done = (bf16[4096,300]{0,1:T(8,128)(2,1)}, bf16[4096,300]{0,1:T(8,128)(2,1)}) async-done(((bf16[4096,300]{0,1:T(8,128)(2,1)}, bf16[4096,300]{0,1:T(8,128)(2,1)}), (bf16[4096,300]{0,1:T(8,128)(2,1)}, bf16[4096,300]{0,1:T(8,128)(2,1)})) %all-reduce.7.cloned.1.call-update) | async-done | bytes 4915216 | tf_op jit(solution)/shard_map/psum | solution.py:27
  184.6 0.0 copy-start.1
  184.6 4.1 %fusion.11 = f32[300,300]{1,0:T(8,128)} fusion(bf16[4096,300]{0,1:T(8,128)(2,1)S(1)} %bitcast_dynamic-update-slice_fusion, bf16[4096,300]{0,1:T(8,128)(2,1)} %get-tuple-element.8), kind=kOutput, calls=%fused_computation.34 | convolution fusion | flops 737280000 | bytes 5275200 | tf_op jit(solution)/shard_map/dot_general | solution.py:49
  188.7 0.0 copy-done.1
  188.7 0.0 copy-start.3
  188.7 2.2 fusion.12
  191.0 0.0 all-reduce.5.cloned.1.call-update
  192.9 0.0 copy-done.3
  192.9 0.1 dynamic-slice_subtract_fusion.1
  193.0 35.9 %all-reduce.5.cloned.1.call-done = (f32[300,300]{1,0:T(8,128)}, f32[300,300]{1,0:T(8,128)}) async-done(((f32[300,300]{1,0:T(8,128)}, f32[300,300]{1,0:T(8,128)}), (f32[300,300]{1,0:T(8,128)}, f32[300,300]{1,0:T(8,128)})) %all-reduce.5.cloned.1.call-update) | async-done | bytes 720016 | tf_op jit(solution)/shard_map/psum | solution.py:52
  228.9 0.0 copy-start
  228.9 0.0 copy-start.2
  228.9 3.4 %fusion.1 = f32[4096,300]{0,1:T(8,128)S(1)} fusion(bf16[4096,300]{0,1:T(8,128)(2,1)} %get-tuple-element.7, f32[300,300]{1,0:T(8,128)} %get-tuple-element.5, f32[300]{0:T(512)S(1)} %get-tuple-element.20, f32[300]{0:T(512)S(1)} %get-tuple-element.19), kind=kOutput, calls=%fused_computation.14 | convolution fusion | flops 737640000 | bytes 7735200 | tf_op jit(solution)/shard_map/dot_general | solution.py:54
  232.4 0.0 copy-done
  232.4 0.0 copy-done.2
  232.4 3.8 %fusion = f32[1,4096,300]{1,2,0:T(8,128)} fusion(f32[4096,300]{0,1:T(8,128)S(1)} %fusion.1, bf16[4096,300]{0,1:T(8,128)(2,1)S(1)} %copy-done, f32[300,300]{1,0:T(8,128)S(1)} %copy-done.2, f32[300]{0:T(512)S(1)} %get-tuple-element.18, f32[300]{0:T(512)S(1)} %get-tuple-element.19), kind=kOutput, calls=%fused_computation.1 | convolution fusion | flops 738868800 | bytes 12650400 | tf_op jit(solution)/shard_map/dot_general | solution.py:54
  236.2 9.7 %copy.5 = f32[1,4096,300]{1,0,2:T(1,128)} copy(f32[1,4096,300]{1,2,0:T(8,128)} %fusion) | data formatting | bytes 9830400 | tf_op jit(solution)/shard_map/broadcast_in_dim | solution.py:57
  (2 shorter events, 0.1 us)
Async XLA Ops:
  6.5 8.9 %copy-start.4 = (s32[2]{0:T(128)S(1)}, s32[2]{0:T(128)}, u32[]{:S(2)}) copy-start(s32[2]{0:T(128)} %param.7) | copy-start | bytes 28
  6.5 178.1 %all-reduce.7.cloned.1.call-start = ((), (), s32[]{:S(2)}) async-start(), calls=%async_computation.1 | async-start | bytes 9961472 | tf_op jit(solution)/shard_map/psum | solution.py:27
  9.5 9.1 %collective-permute-start = (bf16[1,512,300]{1,2,0:T(8,128)(2,1)}, bf16[1,512,300]{1,2,0:T(8,128)(2,1)}, u32[]{:S(2)}, u32[]{:S(2)}) collective-permute-start(bf16[1,512,300]{1,2,0:T(8,128)(2,1)} %get-tuple-element.16), channel_id=1, source_target_pairs={{0,1},{1,0},{4,5},{5,4},{8,9},{9,8},{12,13},{13,12},{2,3},{3,2},{6... | collective-permute-start | bytes 921608 | tf_op jit(solution)/shard_map/ppermute | solution.py:20
  10.0 24.0 %collective-permute-start.1 = (bf16[1,512,300]{1,2,0:T(8,128)(2,1)}, bf16[1,512,300]{1,2,0:T(8,128)(2,1)}, u32[]{:S(2)}, u32[]{:S(2)}) collective-permute-start(bf16[1,512,300]{1,2,0:T(8,128)(2,1)} %get-tuple-element.15), channel_id=1, source_target_pairs={{0,4},{1,5},{4,0},{5,1},{8,12},{9,13},{12,8},{13,9},{2,6},{3,7},{6... | collective-permute-start | bytes 921608 | tf_op jit(solution)/shard_map/ppermute | solution.py:20
  12.6 27.7 %collective-permute-start.2 = (bf16[1,512,300]{1,2,0:T(8,128)(2,1)}, bf16[1,512,300]{1,2,0:T(8,128)(2,1)}, u32[]{:S(2)}, u32[]{:S(2)}) collective-permute-start(bf16[1,512,300]{1,2,0:T(8,128)(2,1)} %get-tuple-element.14), channel_id=1, source_target_pairs={{0,5},{1,4},{4,1},{5,0},{8,13},{9,12},{12,9},{13,8},{2,7},{3,6},{6... | collective-permute-start | bytes 921608 | tf_op jit(solution)/shard_map/ppermute | solution.py:20
  12.7 28.6 %collective-permute-start.3 = (bf16[1,512,300]{1,2,0:T(8,128)(2,1)}, bf16[1,512,300]{1,2,0:T(8,128)(2,1)}, u32[]{:S(2)}, u32[]{:S(2)}) collective-permute-start(bf16[1,512,300]{1,2,0:T(8,128)(2,1)} %get-tuple-element.13), channel_id=1, source_target_pairs={{0,8},{1,9},{4,12},{5,13},{8,0},{9,1},{12,4},{13,5},{2,10},{3,11},... | collective-permute-start | bytes 921608 | tf_op jit(solution)/shard_map/ppermute | solution.py:20
  15.4 26.9 %collective-permute-start.4 = (bf16[1,512,300]{1,2,0:T(8,128)(2,1)S(1)}, bf16[1,512,300]{1,2,0:T(8,128)(2,1)}, u32[]{:S(2)}, u32[]{:S(2)}) collective-permute-start(bf16[1,512,300]{1,2,0:T(8,128)(2,1)S(1)} %get-tuple-element.12), channel_id=1, source_target_pairs={{0,9},{1,8},{4,13},{5,12},{8,1},{9,0},{12,5},{13,4},{2,11},{3,10},... | collective-permute-start | bytes 921608 | tf_op jit(solution)/shard_map/ppermute | solution.py:20
  18.6 31.5 %collective-permute-start.5 = (bf16[1,512,300]{1,2,0:T(8,128)(2,1)S(1)}, bf16[1,512,300]{1,2,0:T(8,128)(2,1)S(1)}, u32[]{:S(2)}, u32[]{:S(2)}) collective-permute-start(bf16[1,512,300]{1,2,0:T(8,128)(2,1)S(1)} %get-tuple-element.17), channel_id=1, source_target_pairs={{0,12},{1,13},{4,8},{5,9},{8,4},{9,5},{12,0},{13,1},{2,14},{3,15},... | collective-permute-start | bytes 921608 | tf_op jit(solution)/shard_map/ppermute | solution.py:20
  33.9 22.1 %collective-permute-start.6 = (bf16[1,512,300]{1,2,0:T(8,128)(2,1)S(1)}, bf16[1,512,300]{1,2,0:T(8,128)(2,1)S(1)}, u32[]{:S(2)}, u32[]{:S(2)}) collective-permute-start(bf16[1,512,300]{1,2,0:T(8,128)(2,1)S(1)} %get-tuple-element.11), channel_id=1, source_target_pairs={{0,13},{1,12},{4,9},{5,8},{8,5},{9,4},{12,1},{13,0},{2,15},{3,14},... | collective-permute-start | bytes 921608 | tf_op jit(solution)/shard_map/ppermute | solution.py:20
  58.7 170.2 %all-reduce.5.cloned.1.call-start = ((), (), s32[]{:S(2)}) async-start(), calls=%async_computation | async-start | bytes 1867776 | tf_op jit(solution)/shard_map/psum | solution.py:52
  184.6 4.1 %copy-start.1 = (bf16[4096,300]{0,1:T(8,128)(2,1)S(1)}, bf16[4096,300]{0,1:T(8,128)(2,1)}, u32[]{:S(2)}) copy-start(bf16[4096,300]{0,1:T(8,128)(2,1)} %get-tuple-element.7) | copy-start | bytes 7372804
  188.7 4.1 %copy-start.3 = (f32[2400]{0:T(1024)S(1)}, f32[2400]{0:T(1024)}, u32[]{:S(2)}) copy-start(f32[2400]{0:T(1024)} %param.6) | copy-start | bytes 28804
  228.9 3.4 %copy-start = (bf16[4096,300]{0,1:T(8,128)(2,1)S(1)}, bf16[4096,300]{0,1:T(8,128)(2,1)}, u32[]{:S(2)}) copy-start(bf16[4096,300]{0,1:T(8,128)(2,1)} %get-tuple-element.8) | copy-start | bytes 7372804
  228.9 3.4 %copy-start.2 = (f32[300,300]{1,0:T(8,128)S(1)}, f32[300,300]{1,0:T(8,128)}, u32[]{:S(2)}) copy-start(f32[300,300]{1,0:T(8,128)} %get-tuple-element.6) | copy-start | bytes 1080004
Sparse Core Ops, SparseCore 0:
  58.9 125.7 all-reduce.6
  191.1 37.7 all-reduce.4
